TPU v7x, 32 devices: a whole 2x2x4 slice. The times are simulated.
32 devices in a mesh: scan: 16 (over z, y, core), row: 2 (over x).
Axes of the slice: x: 2, y: 2, z: 4, core: 2. Of those that a mesh axis runs over, the one named last changes fastest.
Arguments:
- estimate: float32 [128, 64, 512], P('scan', 'row'), may hold values from -6 to 6
- raw: float32 [128, 64, 512], P('scan', 'row'), may hold values from -6 to 6
- offsets: int32 [128], replicated, may hold values from 0 to 16, as said below
- depth_psf: float32 [64], replicated, may hold values from 0.03 to 0.2
- lateral_psf: float32 [17], replicated, may hold values from 0.05 to 0.4
- step_size: float32 [1], replicated, may hold values from 0.3 to 0.8
- threshold: float32 [1], replicated, may hold values from 0.3 to 1.5
Outputs:
- new_estimate: float32 [128, 64, 512], P('scan', 'row')
- misfit: float32 [128, 64, 512], P('scan', 'row')
Inputs may be any that keep to these rules, and one draw needn't show every extreme that they name: offsets[p] is how many planes beyond p the sheet of scan plane p begins; both 0 and 16 occur.
All inputs are finite; a program needn't handle non-finite values.
Results may differ from a plain program's by a relative error of at most 0.0003.
Values sent between devices are 32-bit elements; how exact they have to be, the bound alone decides.
No kernel may reach another device: no remote copies, remote signals or barrier semaphores. Data moves between devices by JAX's collectives and lax.ppermute only.
A program may use at most 64 MiB of HBM per device.

v0:
```python
import jax
import jax.numpy as jnp
from jax import lax
from jax.sharding import PartitionSpec as P

highest_mode = lax.Precision.HIGHEST


def with_halo(cells, axis, width):
    count = lax.axis_size(axis)
    head = lax.slice_in_dim(cells, 0, width, axis=1)
    tail = lax.slice_in_dim(cells, cells.shape[1] - width, cells.shape[1], axis=1)
    zeros = jnp.zeros_like(head)
    if count == 2:
        first = lax.axis_index(axis) == 0
        arrived = lax.ppermute(jnp.where(first, tail, head), axis, [(0, 1), (1, 0)])
        above = jnp.where(first, zeros, arrived)
        below = jnp.where(first, arrived, zeros)
    else:
        ends = count - 1
        above = lax.ppermute(tail, axis, [(i, (i + 1) % count) for i in range(ends)])
        below = lax.ppermute(head, axis, [((i + 1) % count, i) for i in range(ends)])
    return jnp.concatenate([above, cells, below], axis=1)


def band_matrix(kernel_taps, row_count, shift):
    tap_count = kernel_taps.shape[0]
    out_rows = jnp.arange(row_count, dtype=jnp.int32)[:, None]
    in_rows = jnp.arange(row_count + tap_count - 1, dtype=jnp.int32)[None, :]
    lag = shift + in_rows - out_rows
    taps = jnp.arange(tap_count, dtype=jnp.int32)
    return jnp.sum(jnp.where(lag[:, :, None] == taps, kernel_taps, 0.0), axis=-1)


def lateral_apply(band, padded):
    return jnp.einsum("rk,pkc->prc", band, padded, precision=highest_mode)


def sheet_matrix(own_offsets, depth_psf, column_count):
    plane_rows = jnp.arange(own_offsets.shape[0], dtype=jnp.int32)[:, None]
    plane_columns = jnp.arange(column_count, dtype=jnp.int32)[None, :]
    lag_planes = plane_columns - plane_rows - own_offsets[:, None]
    depth_count = depth_psf.shape[0]
    inside = (lag_planes >= 0) & (lag_planes < depth_count)
    taps = jnp.arange(depth_count, dtype=jnp.int32)
    picked = jnp.where(lag_planes[:, :, None] == taps, depth_psf, 0.0)
    return jnp.where(inside, jnp.sum(picked, axis=-1), 0.0)


def transpose_apply(sheet_psf, values):
    return lax.dot_general(sheet_psf, values, (((0,), (0,)), ((), ())), precision=highest_mode)


def body(estimate, raw, offsets, depth_psf, lateral_psf, step_size, threshold):
    plane_count, row_count, width_count = estimate.shape
    flat_count = row_count * width_count
    halo_rows = lateral_psf.shape[0] // 2
    sheet_psf = sheet_matrix(offsets, depth_psf, offsets.shape[0])
    blur_band = band_matrix(lateral_psf, row_count, 0)
    back_band = band_matrix(lateral_psf[::-1], row_count, 0)
    padded = with_halo(estimate, "row", halo_rows)
    blurred = lateral_apply(blur_band, padded).reshape(plane_count, flat_count)
    both_flat = jnp.stack([blurred, raw.reshape(plane_count, flat_count)])
    both_in = lax.all_to_all(both_flat, "scan", split_axis=2, concat_axis=1, tiled=True)
    pencil = both_in[0]
    raw_pencil = both_in[1]
    predicted_pencil = jnp.dot(sheet_psf, pencil, precision=highest_mode)
    misfit_pencil = predicted_pencil - raw_pencil
    back_pencil = transpose_apply(sheet_psf, misfit_pencil)
    both_out = lax.all_to_all(
        jnp.stack([misfit_pencil, back_pencil]), "scan", split_axis=1, concat_axis=2, tiled=True
    )
    misfit = both_out[0]
    back_volume = both_out[1].reshape(plane_count, row_count, width_count)
    padded_back = with_halo(back_volume, "row", halo_rows)
    gradient = lateral_apply(back_band, padded_back)
    stepped = estimate - step_size[0] * gradient
    shrink_level = step_size[0] * threshold[0]
    new_estimate = jnp.sign(stepped) * jnp.maximum(jnp.abs(stepped) - shrink_level, 0.0)
    return (new_estimate, misfit.reshape(plane_count, row_count, width_count))


def solution(mesh):
    placed = (P("scan", "row", None), P("scan", "row", None), P(), P(), P(), P(), P())
    return jax.shard_map(
        body,
        mesh=mesh,
        in_specs=placed,
        out_specs=(P("scan", "row", None), P("scan", "row", None)),
        check_vma=False,
    )
```

profile of v0, /device:TPU:0, one launch (start us, length us, event | category | flops | bytes accessed | tf_op | source)
XLA Modules:
  0.0 181.3 jit_solution(13650661179167656259)
XLA Ops:
  0.6 1.0 slice_select_fusion.1
  1.6 3.0 %collective-permute-start = (f32[8,8,512]{2,1,0:T(8,128)S(1)}, f32[8,8,512]{2,1,0:T(8,128)S(1)}, u32[]{:S(2)}, u32[]{:S(2)}) collective-permute-start(f32[8,8,512]{2,1,0:T(8,128)S(1)} %slice_select_fusion.1), channel_id=1, source_target_pairs={{0,1},{1,0},{2,3},{3,2},{4,5},{5,4},{6,7},{7,6},{8,9},{9,8},{10,11... | collective-permute-start | bytes 393224 | tf_op jit(solution)/shard_map/ppermute | solution.py:16
  4.6 0.7 rev.3
  5.4 1.1 stack_reshape.7
  6.5 0.8 select_reduce_fusion.1
  7.3 0.8 collective-permute-done
  8.2 1.7 convolution_bitcast_fusion.1
  9.9 0.1 stack_reshape.6
  10.0 0.1 pad_maximum_fusion
  10.0 14.6 %copy.19 = f32[2,8,16384]{1,0,2:T(2,128)} copy(f32[2,8,16384]{2,1,0:T(8,128)S(1)} %pad_maximum_fusion) | data formatting | bytes 2097152 | tf_op jit(solution)/shard_map/stack | solution.py:63
  24.6 29.0 %reshape.53 = f32[16,1,16384]{2,1,0:T(1,128)} reshape(f32[16384,2,8]{2,1,0:T(2,128)} %bitcast.42) | data formatting | bytes 2097152
  53.6 6.2 %all-to-all-start = ((f32[16,1,16384]{2,1,0:T(1,128)}), f32[16,1,16384]{2,1,0:T(1,128)S(1)}, u32[]{:S(2)}, u32[]{:S(2)}) async-start(f32[16,1,16384]{2,1,0:T(1,128)} %reshape.53), calls=%async_computation | async-start | bytes 2097152 | tf_op jit(solution)/shard_map/all_to_all | solution.py:64
  59.8 0.1 subtract_subtract_fusion
  59.9 1.4 select_reduce_fusion
  61.3 21.5 %all-to-all-done = f32[16,1,16384]{2,1,0:T(1,128)S(1)} async-done(((f32[16,1,16384]{2,1,0:T(1,128)}), f32[16,1,16384]{2,1,0:T(1,128)S(1)}, u32[]{:S(2)}, u32[]{:S(2)}) %all-to-all-start) | async-done | bytes 1048608 | tf_op jit(solution)/shard_map/all_to_all | solution.py:64
  82.8 0.5 broadcast.33
  83.3 3.1 %reduce = f32[16,16384]{1,0:T(8,128)S(1)} reduce(f32[16,1,16384]{2,1,0:T(1,128)S(1)} %all-to-all-done, f32[]{:T(128)} %broadcast.33), dimensions={1}, to_apply=%all_to_all.22.reduce_sub_computation | reduce | bytes 2097156 | tf_op jit(solution)/shard_map/all_to_all | solution.py:64
  86.4 31.9 %reshape.54 = f32[16384,2,8]{2,1,0:T(2,128)} reshape(f32[16,16384]{1,0:T(8,128)S(1)} %reduce) | data formatting | bytes 2097152
  118.4 20.3 %copy.20 = f32[2,8,16,1024]{3,1,2,0:T(8,128)S(1)} copy(f32[2,8,16,1024]{1,0,3,2:T(2,128)} %bitcast.43) | data formatting | bytes 2097152 | tf_op jit(solution)/shard_map/all_to_all | solution.py:64
  138.7 0.6 convolution_subtract_fusion
  139.3 0.7 convolution_bitcast_fusion
  140.0 0.1 pad_maximum_fusion.1
  140.1 0.8 copy.21
  140.9 0.0 copy-start
  141.0 31.6 %all_to_all.30 = f32[2,128,1024]{2,0,1:T(2,128)S(1)} all-to-all(f32[2,128,1024]{2,0,1:T(2,128)S(1)} %copy.21), channel_id=1, replica_groups=mesh['scan'=16,'row'=2] {'scan'}, dimensions={1} | all-to-all | bytes 2097152 | tf_op jit(solution)/shard_map/all_to_all | solution.py:70
  172.6 0.6 copy.24
  173.2 0.1 fusion.24
  173.3 0.1 reshape_squeeze.6
  173.4 1.6 collective-permute-start.1
  176.3 0.9 reshape_squeeze.7
  177.1 2.5 %collective-permute-done.1 = f32[8,8,512]{2,1,0:T(8,128)S(1)} collective-permute-done((f32[8,8,512]{2,1,0:T(8,128)S(1)}, f32[8,8,512]{2,1,0:T(8,128)S(1)}, u32[]{:S(2)}, u32[]{:S(2)}) %collective-permute-start.1) | collective-permute-done | bytes 131104 | tf_op jit(solution)/shard_map/ppermute | solution.py:16
  179.7 1.6 maximum_multiply_fusion
  (9 shorter events, 0.1 us)
Async XLA Ops:
  1.6 6.5 %collective-permute-start = (f32[8,8,512]{2,1,0:T(8,128)S(1)}, f32[8,8,512]{2,1,0:T(8,128)S(1)}, u32[]{:S(2)}, u32[]{:S(2)}) collective-permute-start(f32[8,8,512]{2,1,0:T(8,128)S(1)} %slice_select_fusion.1), channel_id=1, source_target_pairs={{0,1},{1,0},{2,3},{3,2},{4,5},{5,4},{6,7},{7,6},{8,9},{9,8},{10,11... | collective-permute-start | bytes 393224 | tf_op jit(solution)/shard_map/ppermute | solution.py:16
  24.6 35.2 %copy-start.1 = (s32[128]{0:T(128)S(1)}, s32[128]{0:T(128)}, u32[]{:S(2)}) copy-start(s32[128]{0:T(128)} %param.9) | copy-start | bytes 1540
  24.6 35.3 %copy-start.2 = (f32[64]{0:T(128)S(1)}, f32[64]{0:T(128)}, u32[]{:S(2)}) copy-start(f32[64]{0:T(128)} %param.10) | copy-start | bytes 772
  53.6 29.1 %all-to-all-start = ((f32[16,1,16384]{2,1,0:T(1,128)}), f32[16,1,16384]{2,1,0:T(1,128)S(1)}, u32[]{:S(2)}, u32[]{:S(2)}) async-start(f32[16,1,16384]{2,1,0:T(1,128)} %reshape.53), calls=%async_computation | async-start | bytes 2097152 | tf_op jit(solution)/shard_map/all_to_all | solution.py:64
  140.9 38.7 %copy-start = (f32[8,32,512]{2,1,0:T(8,128)S(1)}, f32[8,32,512]{2,1,0:T(8,128)}, u32[]{:S(2)}) copy-start(f32[8,32,512]{2,1,0:T(8,128)} %param.7) | copy-start | bytes 1572868
  173.4 6.2 %collective-permute-start.1 = (f32[8,8,512]{2,1,0:T(8,128)S(1)}, f32[8,8,512]{2,1,0:T(8,128)S(1)}, u32[]{:S(2)}, u32[]{:S(2)}) collective-permute-start(f32[8,8,512]{2,1,0:T(8,128)S(1)} %slice_select_fusion), channel_id=1, source_target_pairs={{0,1},{1,0},{2,3},{3,2},{4,5},{5,4},{6,7},{7,6},{8,9},{9,8},{10,11... | collective-permute-start | bytes 393224 | tf_op jit(solution)/shard_map/ppermute | solution.py:16
where the time goes:
time: 182 us; the launch traced here: 181 us
  local copies, waits for them, and re-layouts  101 us (55%)
  blocking collectives  31.6 us (17%)
  waiting for transfers between devices  24.8 us (14%)
  starting transfers between devices  10.8 us (6%)
  other arithmetic  6.57 us (4%)
  matrix products  4.67 us (3%)
  between operations  2.12 us (1%)
    unnamed x8, local copies, waits for them, and re-layouts  60.9 us
    all_to_all x1, blocking collectives, body(): lax.all_to_all(jnp.stack([misfit_pencil, back_pencil]), 'scan', split_axi...  31.6 us
    all_to_all x1, waiting for transfers between devices, body(): lax.all_to_all(both_flat, 'scan', split_axis=2, concat_axis=1, tiled=True)  21.5 us
    all_to_all x2, local copies, waits for them, and re-layouts, body(): lax.all_to_all(both_flat, 'scan', split_axis=2, concat_axis=1, tiled=True)  20.8 us
    another operation x3, local copies, waits for them, and re-layouts, body(): both_flat = jnp.stack([blurred, raw.reshape(plane_count, flat_count)])  15.8 us
    all_to_all x1, starting transfers between devices, body(): lax.all_to_all(both_flat, 'scan', split_axis=2, concat_axis=1, tiled=True)  6.2 us
    ppermute x2, starting transfers between devices, with_halo(): arrived = lax.ppermute(jnp.where(first, tail, head), axis, [(0, 1), (1, 0)])  4.56 us
  transfers between devices with their start and end apart: 3, of which 3 were waited for; matrix products, arithmetic and copies ran while one was open for 3% of the time, Pallas kernels for 0%

commit v1 on v0

--- a/solution.py
+++ b/solution.py
@@ -4,6 +4,18 @@
 from jax.sharding import PartitionSpec as P
 
 highest_mode = lax.Precision.HIGHEST
+
+
+def cut_along(x, dim, size):
+    shape = x.shape
+    blocks = x.reshape(*shape[:dim], size, shape[dim] // size, *shape[dim + 1 :])
+    return jnp.moveaxis(blocks, dim, 0)
+
+
+def in_order(blocks, dim):
+    shape = list(blocks.shape[1:])
+    shape[dim] *= blocks.shape[0]
+    return jnp.moveaxis(blocks, 0, dim).reshape(shape)
 
 
 def with_halo(cells, axis, width):
@@ -61,7 +73,14 @@
     padded = with_halo(estimate, "row", halo_rows)
     blurred = lateral_apply(blur_band, padded).reshape(plane_count, flat_count)
     both_flat = jnp.stack([blurred, raw.reshape(plane_count, flat_count)])
-    both_in = lax.all_to_all(both_flat, "scan", split_axis=2, concat_axis=1, tiled=True)
+    peers, place = (lax.axis_size("scan"), lax.axis_index("scan"))
+    blocks = cut_along(both_flat, 2, peers)
+    outs = [blocks[place]]
+    for turn in range(1, peers):
+        sent = blocks[place ^ turn]
+        outs.append(lax.ppermute(sent, "scan", [(i_2, i_2 ^ turn) for i_2 in range(peers)]))
+    blocks = jnp.stack(outs)[place ^ jnp.arange(peers)]
+    both_in = in_order(blocks, 1)
     pencil = both_in[0]
     raw_pencil = both_in[1]
     predicted_pencil = jnp.dot(sheet_psf, pencil, precision=highest_mode)

time: 182 us -> 85.7 us (0.47)
  local copies, waits for them, and re-layouts: 101 us -> 5.85 us
  starting transfers between devices: 10.8 us -> 29.2 us
  waiting for transfers between devices: 24.8 us -> 9.76 us
  other arithmetic: 6.57 us -> 4.07 us
    unnamed x8 -> x39, local copies, waits for them, and re-layouts: 60.9 us -> 0.4 us
    ppermute x0 -> x15, starting transfers between devices: none -> 24.8 us  [body(): lax.ppermute(sent, 'scan', [(i_2, i_2 ^ turn) for i_2 in range(peers)])]
    all_to_all x1 -> x0, waiting for transfers between devices: 21.5 us -> none  [body(): lax.all_to_all(both_flat, 'scan', split_axis=2, concat_axis=1, tiled=True)]
    all_to_all x2 -> x0, local copies, waits for them, and re-layouts: 20.8 us -> none  [body(): lax.all_to_all(both_flat, 'scan', split_axis=2, concat_axis=1, tiled=True)]
    another operation x3, local copies, waits for them, and re-layouts: 15.8 us -> 0.38 us  [body(): both_flat = jnp.stack([blurred, raw.reshape(plane_count, flat_count)])]
    ppermute x0 -> x15, waiting for transfers between devices: none -> 7 us  [body(): lax.ppermute(sent, 'scan', [(i_2, i_2 ^ turn) for i_2 in range(peers)])]
    all_to_all x1 -> x0, starting transfers between devices: 6.2 us -> none  [body(): lax.all_to_all(both_flat, 'scan', split_axis=2, concat_axis=1, tiled=True)]
    all_to_all x1 -> x0, other arithmetic: 3.15 us -> none  [body(): lax.all_to_all(both_flat, 'scan', split_axis=2, concat_axis=1, tiled=True)]
  transfers between devices with their start and end apart: 3 -> 17, of which waited for: 3 -> 6; matrix products, arithmetic and copies ran while one was open for 3% -> 6% of each run, Pallas kernels for 0% -> 0%
where the time goes in v1:
time: 85.7 us; the launch traced here: 85.5 us
  blocking collectives  30.6 us (36%)
  starting transfers between devices  29.2 us (34%)
  waiting for transfers between devices  9.76 us (11%)
  local copies, waits for them, and re-layouts  5.85 us (7%)
  other arithmetic  4.07 us (5%)
  matrix products  3.62 us (4%)
  between operations  2.48 us (3%)
    all_to_all x1, blocking collectives, body(): lax.all_to_all(jnp.stack([misfit_pencil, back_pencil]), 'scan', split_axi...  30.6 us
    ppermute x15, starting transfers between devices, body(): lax.ppermute(sent, 'scan', [(i_2, i_2 ^ turn) for i_2 in range(peers)])  24.8 us
    ppermute x15, waiting for transfers between devices, body(): lax.ppermute(sent, 'scan', [(i_2, i_2 ^ turn) for i_2 in range(peers)])  7 us
    ppermute x2, starting transfers between devices, with_halo(): arrived = lax.ppermute(jnp.where(first, tail, head), axis, [(0, 1), (1, 0)])  4.31 us
    ppermute x2, waiting for transfers between devices, with_halo(): arrived = lax.ppermute(jnp.where(first, tail, head), axis, [(0, 1), (1, 0)])  2.76 us
    dot_general x2, matrix products, lateral_apply(): return jnp.einsum('rk,pkc->prc', band, padded, precision=highest_mode)  2.29 us
    reduce_sum x1, other arithmetic, sheet_matrix(): return jnp.where(inside, jnp.sum(picked, axis=-1), 0.0)  1.99 us
  transfers between devices with their start and end apart: 17, of which 6 were waited for; matrix products, arithmetic and copies ran while one was open for 6% of the time, Pallas kernels for 0%

profile of v1, /device:TPU:0, one launch (start us, length us, event | category | flops | bytes accessed | tf_op | source)
XLA Modules:
  0.0 85.5 jit_solution(11764757607683127562)
XLA Ops:
  0.7 1.1 %slice_select_fusion.1 = f32[8,8,512]{2,1,0:T(8,128)S(1)} fusion(f32[8,32,512]{2,1,0:T(8,128)} %param.7, pred[]{:T(512)S(6)} %eq.20), kind=kLoop, calls=%fused_computation.28 | loop fusion | flops 32768 | bytes 393217 | tf_op jit(solution)/shard_map/jit(_where)/select_n | solution.py:28
  1.7 3.0 %collective-permute-start = (f32[8,8,512]{2,1,0:T(8,128)S(1)}, f32[8,8,512]{2,1,0:T(8,128)S(1)}, u32[]{:S(2)}, u32[]{:S(2)}) collective-permute-start(f32[8,8,512]{2,1,0:T(8,128)S(1)} %slice_select_fusion.1), channel_id=1, source_target_pairs={{0,1},{1,0},{2,3},{3,2},{4,5},{5,4},{6,7},{7,6},{8,9},{9,8},{10,11... | collective-permute-start | bytes 393224 | tf_op jit(solution)/shard_map/ppermute | solution.py:28
  4.8 0.7 subtract_subtract_fusion
  5.5 2.0 %select_reduce_fusion = f32[128,128]{1,0:T(8,128)S(1)} fusion(f32[64]{0:T(128)} %param.10, s32[128,128]{1,0:T(8,128)S(1)} %subtract_subtract_fusion), kind=kLoop, calls=%fused_computation.1 | loop fusion | flops 3129344 | bytes 131328 | tf_op jit(solution)/shard_map/reduce_sum | solution.py:59
  7.6 0.7 rev.3
  8.8 0.6 convolution_bitcast_fusion.1
  9.7 1.3 %constant_dynamic-slice_fusion = (f32[2,8,1,1024]{3,2,1,0:T(1,128)S(1)}, f32[2,8,1,1024]{3,2,1,0:T(1,128)S(1)}, f32[2,8,1,1024]{3,2,1,0:T(1,128)S(1)}, f32[2,8,1...) fusion(f32[2,8,16,1024]{3,2,1,0:T(8,128)S(1)} %constant_dynamic, ...), kind=kLoop, calls=%fused_computation.73 | loop fusion | bytes 2097216 | tf_op jit(solution)/shard_map/dynamic-slice.15
  11.1 1.6 %collective-permute-start.2 = (f32[2,8,1024]{2,1,0:T(8,128)S(1)}, f32[2,8,1024]{2,1,0:T(8,128)S(1)}, u32[]{:S(2)}, u32[]{:S(2)}) collective-permute-start(f32[2,8,1024]{2,1,0:T(8,128)S(1)} %bitcast.135), channel_id=1, source_target_pairs={{0,4},{2,6},{4,0},{6,2},{8,12},{10,14},{12,8},{14,10},{16,20},{18,... | collective-permute-start | bytes 196616 | tf_op jit(solution)/shard_map/ppermute | solution.py:81
  12.7 0.4 collective-permute-start.3
  13.1 1.6 %collective-permute-start.4 = (f32[2,8,1024]{2,1,0:T(8,128)S(1)}, f32[2,8,1024]{2,1,0:T(8,128)S(1)}, u32[]{:S(2)}, u32[]{:S(2)}) collective-permute-start(f32[2,8,1024]{2,1,0:T(8,128)S(1)} %bitcast.133), channel_id=1, source_target_pairs={{0,8},{2,10},{4,12},{6,14},{8,0},{10,2},{12,4},{14,6},{16,24},{18,... | collective-permute-start | bytes 196616 | tf_op jit(solution)/shard_map/ppermute | solution.py:81
  15.2 2.6 %collective-permute-start.6 = (f32[2,8,1024]{2,1,0:T(8,128)S(1)}, f32[2,8,1024]{2,1,0:T(8,128)S(1)}, u32[]{:S(2)}, u32[]{:S(2)}) collective-permute-start(f32[2,8,1024]{2,1,0:T(8,128)S(1)} %bitcast.131), channel_id=1, source_target_pairs={{0,12},{2,14},{4,8},{6,10},{8,4},{10,6},{12,0},{14,2},{16,28},{18,... | collective-permute-start | bytes 196616 | tf_op jit(solution)/shard_map/ppermute | solution.py:81
  18.1 2.7 %collective-permute-start.8 = (f32[2,8,1024]{2,1,0:T(8,128)S(1)}, f32[2,8,1024]{2,1,0:T(8,128)S(1)}, u32[]{:S(2)}, u32[]{:S(2)}) collective-permute-start(f32[2,8,1024]{2,1,0:T(8,128)S(1)} %bitcast.129), channel_id=1, source_target_pairs={{0,16},{2,18},{4,20},{6,22},{8,24},{10,26},{12,28},{14,30},{16,0},... | collective-permute-start | bytes 196616 | tf_op jit(solution)/shard_map/ppermute | solution.py:81
  20.7 0.4 collective-permute-start.9
  21.2 3.2 %collective-permute-start.10 = (f32[2,8,1024]{2,1,0:T(8,128)S(1)}, f32[2,8,1024]{2,1,0:T(8,128)S(1)}, u32[]{:S(2)}, u32[]{:S(2)}) collective-permute-start(f32[2,8,1024]{2,1,0:T(8,128)S(1)} %bitcast.127), channel_id=1, source_target_pairs={{0,20},{2,22},{4,16},{6,18},{8,28},{10,30},{12,24},{14,26},{16,4},... | collective-permute-start | bytes 196616 | tf_op jit(solution)/shard_map/ppermute | solution.py:81
  24.6 3.6 %collective-permute-start.12 = (f32[2,8,1024]{2,1,0:T(8,128)S(1)}, f32[2,8,1024]{2,1,0:T(8,128)S(1)}, u32[]{:S(2)}, u32[]{:S(2)}) collective-permute-start(f32[2,8,1024]{2,1,0:T(8,128)S(1)} %bitcast.125), channel_id=1, source_target_pairs={{0,24},{2,26},{4,28},{6,30},{8,16},{10,18},{12,20},{14,22},{16,8},... | collective-permute-start | bytes 196616 | tf_op jit(solution)/shard_map/ppermute | solution.py:81
  28.2 3.7 %collective-permute-start.13 = (f32[2,8,1024]{2,1,0:T(8,128)S(1)}, f32[2,8,1024]{2,1,0:T(8,128)S(1)}, u32[]{:S(2)}, u32[]{:S(2)}) collective-permute-start(f32[2,8,1024]{2,1,0:T(8,128)S(1)} %bitcast.124), channel_id=1, source_target_pairs={{0,26},{2,24},{4,30},{6,28},{8,18},{10,16},{12,22},{14,20},{16,10}... | collective-permute-start | bytes 196616 | tf_op jit(solution)/shard_map/ppermute | solution.py:81
  31.9 0.6 collective-permute-done.9
  32.6 3.6 %collective-permute-start.14 = (f32[2,8,1024]{2,1,0:T(8,128)S(1)}, f32[2,8,1024]{2,1,0:T(8,128)S(1)}, u32[]{:S(2)}, u32[]{:S(2)}) collective-permute-start(f32[2,8,1024]{2,1,0:T(8,128)S(1)} %bitcast.123), channel_id=1, source_target_pairs={{0,28},{2,30},{4,24},{6,26},{8,20},{10,22},{12,16},{14,18},{16,12}... | collective-permute-start | bytes 196616 | tf_op jit(solution)/shard_map/ppermute | solution.py:81
  36.4 0.8 collective-permute-start.15
  37.2 0.6 collective-permute-done.11
  37.8 2.0 %collective-permute-done.14 = f32[2,8,1024]{2,1,0:T(8,128)S(1)} collective-permute-done((f32[2,8,1024]{2,1,0:T(8,128)S(1)}, f32[2,8,1024]{2,1,0:T(8,128)S(1)}, u32[]{:S(2)}, u32[]{:S(2)}) %collective-permute-start.14) | collective-permute-done | bytes 65568 | tf_op jit(solution)/shard_map/ppermute | solution.py:81
  39.9 3.5 %collective-permute-done.15 = f32[2,8,1024]{2,1,0:T(8,128)S(1)} collective-permute-done((f32[2,8,1024]{2,1,0:T(8,128)S(1)}, f32[2,8,1024]{2,1,0:T(8,128)S(1)}, u32[]{:S(2)}, u32[]{:S(2)}) %collective-permute-start.15) | collective-permute-done | bytes 65568 | tf_op jit(solution)/shard_map/ppermute | solution.py:81
  43.3 0.6 gather_fusion
  44.0 0.6 convolution_subtract_fusion
  44.6 0.7 convolution_bitcast_fusion
  45.4 0.8 copy.13
  46.2 30.6 %all_to_all.15 = f32[2,128,1024]{2,0,1:T(2,128)S(1)} all-to-all(f32[2,128,1024]{2,0,1:T(2,128)S(1)} %copy.13), channel_id=1, replica_groups=mesh['scan'=16,'row'=2] {'scan'}, dimensions={1} | all-to-all | bytes 2097152 | tf_op jit(solution)/shard_map/all_to_all | solution.py:89
  76.8 0.6 copy.48
  77.6 1.3 %collective-permute-start.16 = (f32[8,8,512]{2,1,0:T(8,128)S(1)}, f32[8,8,512]{2,1,0:T(8,128)S(1)}, u32[]{:S(2)}, u32[]{:S(2)}) collective-permute-start(f32[8,8,512]{2,1,0:T(8,128)S(1)} %slice_select_fusion), channel_id=1, source_target_pairs={{0,1},{1,0},{2,3},{3,2},{4,5},{5,4},{6,7},{7,6},{8,9},{9,8},{10,11... | collective-permute-start | bytes 393224 | tf_op jit(solution)/shard_map/ppermute | solution.py:28
  80.2 0.9 %reshape_squeeze.7 = f32[8,32,512]{2,1,0:T(8,128)} reshape(f32[1,8,16,1024]{3,2,1,0:T(8,128)S(1)} %get-tuple-element.4) | data formatting | bytes 1048576 | tf_op jit(solution)/shard_map/reshape;squeeze | solution.py:99
  81.1 2.8 %collective-permute-done.16 = f32[8,8,512]{2,1,0:T(8,128)S(1)} collective-permute-done((f32[8,8,512]{2,1,0:T(8,128)S(1)}, f32[8,8,512]{2,1,0:T(8,128)S(1)}, u32[]{:S(2)}, u32[]{:S(2)}) %collective-permute-start.16) | collective-permute-done | bytes 131104 | tf_op jit(solution)/shard_map/ppermute | solution.py:28
  83.9 1.6 %maximum_multiply_fusion = f32[8,32,512]{2,1,0:T(8,128)} fusion(f32[8,32,512]{2,1,0:T(8,128)S(1)} %copy-done, f32[8,8,512]{2,1,0:T(8,128)S(1)} %get-tuple-element.23, f32[8,32,512]{2,1,0:T(8,128)S(1)} %reshape_squeeze.6, f32[8,8,512]{2,1,0:T(8,128)S(1)} %get-tuple-element.22, f32[]{:T(128)S(6)} %mul.18, f32[]{:T(128)} %bitcast.115, ...), kind=kOutput, calls=%fused_computation.23 | convolution fusion | flops 76808192 | bytes 1841160 | tf_op jit(solution)/shard_map/rk,pkc->prc/dot_general | solution.py:48
  (69 shorter events, 2.2 us)
Async XLA Ops:
  0.6 8.0 %copy-start.3 = (f32[17]{0:T(128)S(1)}, f32[17]{0:T(128)}, u32[]{:S(2)}) copy-start(f32[17]{0:T(128)} %param.11) | copy-start | bytes 208
  0.6 7.7 %copy-start.1 = (f32[8,32,512]{2,1,0:T(8,128)S(1)}, f32[8,32,512]{2,1,0:T(8,128)}, u32[]{:S(2)}) copy-start(f32[8,32,512]{2,1,0:T(8,128)} %param.8) | copy-start | bytes 1572868
  0.7 8.1 %copy-start = (f32[8,32,512]{2,1,0:T(8,128)S(1)}, f32[8,32,512]{2,1,0:T(8,128)}, u32[]{:S(2)}) copy-start(f32[8,32,512]{2,1,0:T(8,128)} %param.7) | copy-start | bytes 1572868
  1.7 7.0 %collective-permute-start = (f32[8,8,512]{2,1,0:T(8,128)S(1)}, f32[8,8,512]{2,1,0:T(8,128)S(1)}, u32[]{:S(2)}, u32[]{:S(2)}) collective-permute-start(f32[8,8,512]{2,1,0:T(8,128)S(1)} %slice_select_fusion.1), channel_id=1, source_target_pairs={{0,1},{1,0},{2,3},{3,2},{4,5},{5,4},{6,7},{7,6},{8,9},{9,8},{10,11... | collective-permute-start | bytes 393224 | tf_op jit(solution)/shard_map/ppermute | solution.py:28
  11.0 4.1 %collective-permute-start.1 = (f32[2,8,1024]{2,1,0:T(8,128)S(1)}, f32[2,8,1024]{2,1,0:T(8,128)S(1)}, u32[]{:S(2)}, u32[]{:S(2)}) collective-permute-start(f32[2,8,1024]{2,1,0:T(8,128)S(1)} %bitcast.136), channel_id=1, source_target_pairs={{0,2},{2,0},{4,6},{6,4},{8,10},{10,8},{12,14},{14,12},{16,18},{18,... | collective-permute-start | bytes 196616 | tf_op jit(solution)/shard_map/ppermute | solution.py:81
  11.1 6.6 %collective-permute-start.2 = (f32[2,8,1024]{2,1,0:T(8,128)S(1)}, f32[2,8,1024]{2,1,0:T(8,128)S(1)}, u32[]{:S(2)}, u32[]{:S(2)}) collective-permute-start(f32[2,8,1024]{2,1,0:T(8,128)S(1)} %bitcast.135), channel_id=1, source_target_pairs={{0,4},{2,6},{4,0},{6,2},{8,12},{10,14},{12,8},{14,10},{16,20},{18,... | collective-permute-start | bytes 196616 | tf_op jit(solution)/shard_map/ppermute | solution.py:81
  12.7 5.3 %collective-permute-start.3 = (f32[2,8,1024]{2,1,0:T(8,128)S(1)}, f32[2,8,1024]{2,1,0:T(8,128)S(1)}, u32[]{:S(2)}, u32[]{:S(2)}) collective-permute-start(f32[2,8,1024]{2,1,0:T(8,128)S(1)} %bitcast.134), channel_id=1, source_target_pairs={{0,6},{2,4},{4,2},{6,0},{8,14},{10,12},{12,10},{14,8},{16,22},{18,... | collective-permute-start | bytes 196616 | tf_op jit(solution)/shard_map/ppermute | solution.py:81
  13.1 7.6 %collective-permute-start.4 = (f32[2,8,1024]{2,1,0:T(8,128)S(1)}, f32[2,8,1024]{2,1,0:T(8,128)S(1)}, u32[]{:S(2)}, u32[]{:S(2)}) collective-permute-start(f32[2,8,1024]{2,1,0:T(8,128)S(1)} %bitcast.133), channel_id=1, source_target_pairs={{0,8},{2,10},{4,12},{6,14},{8,0},{10,2},{12,4},{14,6},{16,24},{18,... | collective-permute-start | bytes 196616 | tf_op jit(solution)/shard_map/ppermute | solution.py:81
  14.8 6.4 %collective-permute-start.5 = (f32[2,8,1024]{2,1,0:T(8,128)S(1)}, f32[2,8,1024]{2,1,0:T(8,128)S(1)}, u32[]{:S(2)}, u32[]{:S(2)}) collective-permute-start(f32[2,8,1024]{2,1,0:T(8,128)S(1)} %bitcast.132), channel_id=1, source_target_pairs={{0,10},{2,8},{4,14},{6,12},{8,2},{10,0},{12,6},{14,4},{16,26},{18,... | collective-permute-start | bytes 196616 | tf_op jit(solution)/shard_map/ppermute | solution.py:81
  15.2 9.2 %collective-permute-start.6 = (f32[2,8,1024]{2,1,0:T(8,128)S(1)}, f32[2,8,1024]{2,1,0:T(8,128)S(1)}, u32[]{:S(2)}, u32[]{:S(2)}) collective-permute-start(f32[2,8,1024]{2,1,0:T(8,128)S(1)} %bitcast.131), channel_id=1, source_target_pairs={{0,12},{2,14},{4,8},{6,10},{8,4},{10,6},{12,0},{14,2},{16,28},{18,... | collective-permute-start | bytes 196616 | tf_op jit(solution)/shard_map/ppermute | solution.py:81
  17.8 6.8 %collective-permute-start.7 = (f32[2,8,1024]{2,1,0:T(8,128)S(1)}, f32[2,8,1024]{2,1,0:T(8,128)S(1)}, u32[]{:S(2)}, u32[]{:S(2)}) collective-permute-start(f32[2,8,1024]{2,1,0:T(8,128)S(1)} %bitcast.130), channel_id=1, source_target_pairs={{0,14},{2,12},{4,10},{6,8},{8,6},{10,4},{12,2},{14,0},{16,30},{18,... | collective-permute-start | bytes 196616 | tf_op jit(solution)/shard_map/ppermute | solution.py:81
  18.1 10.2 %collective-permute-start.8 = (f32[2,8,1024]{2,1,0:T(8,128)S(1)}, f32[2,8,1024]{2,1,0:T(8,128)S(1)}, u32[]{:S(2)}, u32[]{:S(2)}) collective-permute-start(f32[2,8,1024]{2,1,0:T(8,128)S(1)} %bitcast.129), channel_id=1, source_target_pairs={{0,16},{2,18},{4,20},{6,22},{8,24},{10,26},{12,28},{14,30},{16,0},... | collective-permute-start | bytes 196616 | tf_op jit(solution)/shard_map/ppermute | solution.py:81
  20.7 11.8 %collective-permute-start.9 = (f32[2,8,1024]{2,1,0:T(8,128)S(1)}, f32[2,8,1024]{2,1,0:T(8,128)S(1)}, u32[]{:S(2)}, u32[]{:S(2)}) collective-permute-start(f32[2,8,1024]{2,1,0:T(8,128)S(1)} %bitcast.128), channel_id=1, source_target_pairs={{0,18},{2,16},{4,22},{6,20},{8,26},{10,24},{12,30},{14,28},{16,2},... | collective-permute-start | bytes 196616 | tf_op jit(solution)/shard_map/ppermute | solution.py:81
  21.2 15.2 %collective-permute-start.10 = (f32[2,8,1024]{2,1,0:T(8,128)S(1)}, f32[2,8,1024]{2,1,0:T(8,128)S(1)}, u32[]{:S(2)}, u32[]{:S(2)}) collective-permute-start(f32[2,8,1024]{2,1,0:T(8,128)S(1)} %bitcast.127), channel_id=1, source_target_pairs={{0,20},{2,22},{4,16},{6,18},{8,28},{10,30},{12,24},{14,26},{16,4},... | collective-permute-start | bytes 196616 | tf_op jit(solution)/shard_map/ppermute | solution.py:81
  24.4 13.4 %collective-permute-start.11 = (f32[2,8,1024]{2,1,0:T(8,128)S(1)}, f32[2,8,1024]{2,1,0:T(8,128)S(1)}, u32[]{:S(2)}, u32[]{:S(2)}) collective-permute-start(f32[2,8,1024]{2,1,0:T(8,128)S(1)} %bitcast.126), channel_id=1, source_target_pairs={{0,22},{2,20},{4,18},{6,16},{8,30},{10,28},{12,26},{14,24},{16,6},... | collective-permute-start | bytes 196616 | tf_op jit(solution)/shard_map/ppermute | solution.py:81
  24.6 13.2 %collective-permute-start.12 = (f32[2,8,1024]{2,1,0:T(8,128)S(1)}, f32[2,8,1024]{2,1,0:T(8,128)S(1)}, u32[]{:S(2)}, u32[]{:S(2)}) collective-permute-start(f32[2,8,1024]{2,1,0:T(8,128)S(1)} %bitcast.125), channel_id=1, source_target_pairs={{0,24},{2,26},{4,28},{6,30},{8,16},{10,18},{12,20},{14,22},{16,8},... | collective-permute-start | bytes 196616 | tf_op jit(solution)/shard_map/ppermute | solution.py:81
  28.2 9.6 %collective-permute-start.13 = (f32[2,8,1024]{2,1,0:T(8,128)S(1)}, f32[2,8,1024]{2,1,0:T(8,128)S(1)}, u32[]{:S(2)}, u32[]{:S(2)}) collective-permute-start(f32[2,8,1024]{2,1,0:T(8,128)S(1)} %bitcast.124), channel_id=1, source_target_pairs={{0,26},{2,24},{4,30},{6,28},{8,18},{10,16},{12,22},{14,20},{16,10}... | collective-permute-start | bytes 196616 | tf_op jit(solution)/shard_map/ppermute | solution.py:81
  32.6 7.3 %collective-permute-start.14 = (f32[2,8,1024]{2,1,0:T(8,128)S(1)}, f32[2,8,1024]{2,1,0:T(8,128)S(1)}, u32[]{:S(2)}, u32[]{:S(2)}) collective-permute-start(f32[2,8,1024]{2,1,0:T(8,128)S(1)} %bitcast.123), channel_id=1, source_target_pairs={{0,28},{2,30},{4,24},{6,26},{8,20},{10,22},{12,16},{14,18},{16,12}... | collective-permute-start | bytes 196616 | tf_op jit(solution)/shard_map/ppermute | solution.py:81
  36.4 6.9 %collective-permute-start.15 = (f32[2,8,1024]{2,1,0:T(8,128)S(1)}, f32[2,8,1024]{2,1,0:T(8,128)S(1)}, u32[]{:S(2)}, u32[]{:S(2)}) collective-permute-start(f32[2,8,1024]{2,1,0:T(8,128)S(1)} %bitcast.122), channel_id=1, source_target_pairs={{0,30},{2,28},{4,26},{6,24},{8,22},{10,20},{12,18},{14,16},{16,14}... | collective-permute-start | bytes 196616 | tf_op jit(solution)/shard_map/ppermute | solution.py:81
  43.3 0.7 copy-start.2
  77.6 6.2 %collective-permute-start.16 = (f32[8,8,512]{2,1,0:T(8,128)S(1)}, f32[8,8,512]{2,1,0:T(8,128)S(1)}, u32[]{:S(2)}, u32[]{:S(2)}) collective-permute-start(f32[8,8,512]{2,1,0:T(8,128)S(1)} %slice_select_fusion), channel_id=1, source_target_pairs={{0,1},{1,0},{2,3},{3,2},{4,5},{5,4},{6,7},{7,6},{8,9},{9,8},{10,11... | collective-permute-start | bytes 393224 | tf_op jit(solution)/shard_map/ppermute | solution.py:28
